TPU v7x, 512 devices: a whole 4x8x8 slice. The times are simulated.
512 devices in a mesh: row: 64 (over x, y, core), col: 8 (over z).
Axes of the slice: x: 4, y: 8, z: 8, core: 2. Of those that a mesh axis runs over, the one named last changes fastest.
Arguments:
- grad_out: bfloat16 [2048, 12288], P('row', 'col'), may hold values from -3.5 to 3.5
- pre_act: bfloat16 [2048, 24576], P('col', 'row'), may hold values from -6 to 6
- down_weight: bfloat16 [24576, 12288], P('row', 'col'), may hold values from -0.0546875 to 0.0546875
Outputs:
- grad_pre: bfloat16 [2048, 24576], P('col', 'row')
- grad_weight: bfloat16 [24576, 12288], P('row', 'col')
All inputs are finite; a program needn't handle non-finite values.
Results may differ from a plain program's by a relative error of at most 0.015.
Values may be sent and summed in bfloat16 or wider, within the bound.
No kernel may reach another device: no remote copies, remote signals or barrier semaphores. Data moves between devices by JAX's collectives and lax.ppermute only.
A program may use at most 64 MiB of HBM per device.

v0:
```python
import jax
import jax.numpy as jnp
from jax import lax
from jax.sharding import PartitionSpec as P

coef = 0.7978845608
cubic = 0.044715


def gelu_fwd(x):
    return 0.5 * x * (1.0 + jnp.tanh(coef * (x + cubic * x * x * x)))


def gelu_grad(x):
    inner = coef * (x + cubic * x * x * x)
    tangent = jnp.tanh(inner)
    return 0.5 * (1.0 + tangent) + 0.5 * x * (1.0 - tangent * tangent) * coef * (
        1.0 + 3.0 * cubic * x * x
    )


def body(grad_out, pre_act, down_weight):
    grad_all = lax.all_gather(grad_out, "row", axis=0, tiled=True)
    pre_all = lax.all_gather(pre_act, "col", axis=0, tiled=True)
    hidden = gelu_fwd(pre_all.astype(jnp.float32)).astype(jnp.bfloat16)
    grad_weight = lax.dot_general(
        hidden, grad_all, (((0,), (0,)), ((), ())), preferred_element_type=jnp.float32
    ).astype(jnp.bfloat16)
    partial_term = lax.dot_general(
        grad_all, down_weight, (((1,), (1,)), ((), ())), preferred_element_type=jnp.float32
    )
    grad_hidden = lax.psum_scatter(
        partial_term.astype(jnp.bfloat16), "col", scatter_dimension=0, tiled=True
    ).astype(jnp.float32)
    grad_pre = (grad_hidden * gelu_grad(pre_act.astype(jnp.float32))).astype(jnp.bfloat16)
    return (grad_pre, grad_weight)


def solution(mesh):
    in_specs = (P("row", "col"), P("col", "row"), P("row", "col"))
    out_specs = (P("col", "row"), P("row", "col"))
    return jax.shard_map(body, mesh=mesh, in_specs=in_specs, out_specs=out_specs, check_vma=False)
```

profile of v0, /device:TPU:2, one launch (start us, length us, event | category | flops | bytes accessed | tf_op | source)
XLA Modules:
  0.0 197.5 jit_solution(17193629523569997921)
XLA Ops:
  7.2 0.0 copy-start
  7.2 0.0 all-gather.3.cloned.1.call-start
  7.2 0.7 all-gather.3.cloned.1.call-update
  7.9 0.0 all-gather.5.cloned.1.call-start
  8.0 0.7 all-gather.5.cloned.1.call-update
  8.7 0.0 reduce-scatter.2.cloned.1.call-start
  8.7 91.8 %all-gather.3.cloned.1.call-done = bf16[2048,1536]{1,0:T(8,128)(2,1)} async-done(((bf16[32,1536]{1,0:T(8,128)(2,1)}), bf16[2048,1536]{1,0:T(8,128)(2,1)}) %all-gather.3.cloned.1.call-update) | async-done | bytes 6291472 | tf_op jit(solution)/shard_map/all_gather | solution.py:23
  100.5 0.0 copy-done
  100.5 7.5 %convolution_convert_fusion.1 = bf16[2048,384]{1,0:T(8,128)(2,1)} fusion(bf16[2048,1536]{1,0:T(8,128)(2,1)} %all-gather.3.cloned.1.call-done, bf16[384,1536]{1,0:T(8,128)(2,1)S(1)} %copy-done), kind=kOutput, calls=%fused_computation.11 | convolution fusion | flops 2416705536 | bytes 9043968 | tf_op jit(solution)/shard_map/dot_general | solution.py:29
  108.0 0.0 reduce-scatter.2.cloned.1.call-update
  108.0 0.0 copy-start.1
  108.0 35.9 %all-gather.5.cloned.1.call-done = bf16[2048,384]{1,0:T(8,128)(2,1)} async-done(((bf16[256,384]{1,0:T(8,128)(2,1)}), bf16[2048,384]{1,0:T(8,128)(2,1)}) %all-gather.5.cloned.1.call-update) | async-done | bytes 1572880 | tf_op jit(solution)/shard_map/all_gather | solution.py:24
  143.9 7.0 %convolution_convert_fusion = bf16[384,1536]{1,0:T(8,128)(2,1)} fusion(bf16[2048,1536]{1,0:T(8,128)(2,1)} %all-gather.3.cloned.1.call-done, bf16[2048,384]{1,0:T(8,128)(2,1)} %all-gather.5.cloned.1.call-done), kind=kOutput, calls=%fused_computation.10 | convolution fusion | flops 2424373248 | bytes 9043968 | tf_op jit(solution)/shard_map/dot_general | solution.py:26
  150.9 38.2 %reduce-scatter.2.cloned.1.call-done = bf16[256,384]{1,0:T(8,128)(2,1)} async-done(((bf16[2048,384]{1,0:T(8,128)(2,1)}), bf16[256,384]{1,0:T(8,128)(2,1)}) %reduce-scatter.2.cloned.1.call-update) | async-done | bytes 196624 | tf_op jit(solution)/shard_map/reduce_scatter | solution.py:32
  189.1 0.0 copy-done.1
  189.1 1.9 fusion.17
Async XLA Ops:
  7.2 93.3 %copy-start = (bf16[384,1536]{1,0:T(8,128)(2,1)S(1)}, bf16[384,1536]{1,0:T(8,128)(2,1)}, u32[]{:S(2)}) copy-start(bf16[384,1536]{1,0:T(8,128)(2,1)} %param.5) | copy-start | bytes 3538948
  7.2 93.3 %all-gather.3.cloned.1.call-start = ((), (), s32[]{:S(2)}) async-start(), calls=%async_computation.1 | async-start | bytes 6389760 | tf_op jit(solution)/shard_map/all_gather | solution.py:23
  7.9 136.0 %all-gather.5.cloned.1.call-start = ((), (), s32[]{:S(2)}) async-start(), calls=%async_computation.3 | async-start | bytes 1769472 | tf_op jit(solution)/shard_map/all_gather | solution.py:24
  8.7 180.4 %reduce-scatter.2.cloned.1.call-start = ((), (), s32[]{:S(2)}) async-start(), calls=%async_computation.2 | async-start | bytes 1769472 | tf_op jit(solution)/shard_map/reduce_scatter | solution.py:32
  108.0 81.1 %copy-start.1 = (bf16[256,384]{1,0:T(8,128)(2,1)S(1)}, bf16[256,384]{1,0:T(8,128)(2,1)}, u32[]{:S(2)}) copy-start(bf16[256,384]{1,0:T(8,128)(2,1)} %param.4) | copy-start | bytes 589828
Sparse Core Ops, SparseCore 0:
  11.3 89.1 all-gather.2
  102.6 41.3 all-gather.4
  146.8 42.2 reduce-scatter.1
where the time goes:
time: 198 us; the launch traced here: 197 us
  waiting for transfers between devices  167 us (84%)
  matrix products  14.5 us (7%)
  between operations  13.8 us (7%)
    all_gather x1, waiting for transfers between devices, body(): grad_all = lax.all_gather(grad_out, 'row', axis=0, tiled=True)  91.8 us
    reduce_scatter x1, waiting for transfers between devices, body(): lax.psum_scatter(partial_term.astype(jnp.bfloat16), 'col', scatter_dimens...  38.2 us
    all_gather x1, waiting for transfers between devices, body(): pre_all = lax.all_gather(pre_act, 'col', axis=0, tiled=True)  35.9 us
    dot_general x1, matrix products, body(): lax.dot_general(grad_all, down_weight, (((1,), (1,)), ((), ())), preferre...  7.48 us
    dot_general x1, matrix products, body(): lax.dot_general(hidden, grad_all, (((0,), (0,)), ((), ())), preferred_ele...  6.99 us
  transfers between devices with their start and end apart: 3, of which 3 were waited for; matrix products, arithmetic and copies ran while one was open for 7% of the time, Pallas kernels for 0%

commit v1 on v0

--- a/solution.py
+++ b/solution.py
@@ -21,7 +21,16 @@
 
 def body(grad_out, pre_act, down_weight):
     grad_all = lax.all_gather(grad_out, "row", axis=0, tiled=True)
-    pre_all = lax.all_gather(pre_act, "col", axis=0, tiled=True)
+    ways = lax.axis_size("col")
+    up = [(d, (d + 1) % ways) for d in range(ways)]
+    down = [(d, (d - 1) % ways) for d in range(ways)]
+    earlier, later = ([pre_act], [pre_act])
+    for _ in range(ways // 2):
+        earlier.append(lax.ppermute(earlier[-1], "col", up))
+    for _ in range((ways - 1) // 2):
+        later.append(lax.ppermute(later[-1], "col", down))
+    line = jnp.concatenate([*earlier[::-1], *later[1:]], axis=0)
+    pre_all = jnp.roll(line, (lax.axis_index("col") - ways // 2) * pre_act.shape[0], axis=0)
     hidden = gelu_fwd(pre_all.astype(jnp.float32)).astype(jnp.bfloat16)
     grad_weight = lax.dot_general(
         hidden, grad_all, (((0,), (0,)), ((), ())), preferred_element_type=jnp.float32

time: 198 us -> 162 us (0.82)
  the two profiles are of different devices: /device:TPU:2 before, /device:TPU:34 now
where the time goes in v1:
time: 162 us
  waiting for transfers between devices  104 us (64%)
  starting transfers between devices  27.1 us (17%)
  between operations  14.3 us (9%)
  matrix products  14 us (9%)
  other arithmetic  1.88 us (1%)
    all_gather x1, waiting for transfers between devices, body(): grad_all = lax.all_gather(grad_out, 'row', axis=0, tiled=True)  71.5 us
    ppermute x3, starting transfers between devices, body(): later.append(lax.ppermute(later[-1], 'col', down))  17 us
    ppermute x3, waiting for transfers between devices, body(): later.append(lax.ppermute(later[-1], 'col', down))  14.2 us
    ppermute x4, waiting for transfers between devices, body(): earlier.append(lax.ppermute(earlier[-1], 'col', up))  12.7 us
    ppermute x4, starting transfers between devices, body(): earlier.append(lax.ppermute(earlier[-1], 'col', up))  10 us
    dot_general x1, matrix products, body(): lax.dot_general(grad_all, down_weight, (((1,), (1,)), ((), ())), preferre...  7.39 us
    dot_general x1, matrix products, body(): lax.dot_general(hidden, grad_all, (((0,), (0,)), ((), ())), preferred_ele...  6.57 us
    reduce_scatter x1, waiting for transfers between devices, body(): lax.psum_scatter(partial_term.astype(jnp.bfloat16), 'col', scatter_dimens...  5.17 us
  transfers between devices with their start and end apart: 9, of which 7 were waited for; matrix products, arithmetic and copies ran while one was open for 9% of the time, Pallas kernels for 0%

profile of v1, /device:TPU:34, one launch (start us, length us, event | category | flops | bytes accessed | tf_op | source)
XLA Modules:
  0.0 162.1 jit_solution(13570324043581957179)
XLA Ops:
  7.2 0.0 copy-start
  7.2 0.0 all-gather.2.cloned.1.call-start
  7.2 0.7 all-gather.2.cloned.1.call-update
  7.9 0.0 copy-start.1
  7.9 0.0 reduce-scatter.2.cloned.1.call-start
  8.0 4.3 %collective-permute-start = (bf16[256,384]{1,0:T(8,128)(2,1)}, bf16[256,384]{1,0:T(8,128)(2,1)S(1)}, u32[]{:S(2)}, u32[]{:S(2)}) collective-permute-start(bf16[256,384]{1,0:T(8,128)(2,1)} %param.4), channel_id=1, source_target_pairs={{0,1},{1,2},{2,3},{3,4},{4,5},{5,6},{6,7},{7,0},{8,9},{9,10},{10,1... | collective-permute-start | bytes 589832 | tf_op jit(solution)/shard_map/ppermute | solution.py:29
  12.3 11.8 %collective-permute-done = bf16[256,384]{1,0:T(8,128)(2,1)S(1)} collective-permute-done((bf16[256,384]{1,0:T(8,128)(2,1)}, bf16[256,384]{1,0:T(8,128)(2,1)S(1)}, u32[]{:S(2)}, u32[]{:S(2)}) %collective-permute-start) | collective-permute-done | bytes 196640 | tf_op jit(solution)/shard_map/ppermute | solution.py:29
  24.0 1.9 %collective-permute-start.1 = (bf16[256,384]{1,0:T(8,128)(2,1)S(1)}, bf16[256,384]{1,0:T(8,128)(2,1)S(1)}, u32[]{:S(2)}, u32[]{:S(2)}) collective-permute-start(bf16[256,384]{1,0:T(8,128)(2,1)S(1)} %collective-permute-done), channel_id=1, source_target_pairs={{0,1},{1,2},{2,3},{3,4},{4,5},{5,6},{6,7},{7,0},{8,9},{9,10},{10,1... | collective-permute-start | bytes 589832 | tf_op jit(solution)/shard_map/ppermute | solution.py:29
  25.9 71.5 %all-gather.2.cloned.1.call-done = bf16[2048,1536]{1,0:T(8,128)(2,1)} async-done(((bf16[32,1536]{1,0:T(8,128)(2,1)}), bf16[2048,1536]{1,0:T(8,128)(2,1)}) %all-gather.2.cloned.1.call-update) | async-done | bytes 6291472 | tf_op jit(solution)/shard_map/all_gather | solution.py:23
  97.4 0.0 copy-done
  97.4 7.4 %convolution_convert_fusion.1 = bf16[2048,384]{1,0:T(8,128)(2,1)} fusion(bf16[2048,1536]{1,0:T(8,128)(2,1)} %all-gather.2.cloned.1.call-done, bf16[384,1536]{1,0:T(8,128)(2,1)S(1)} %copy-done), kind=kOutput, calls=%fused_computation.11 | convolution fusion | flops 2416705536 | bytes 9043968 | tf_op jit(solution)/shard_map/dot_general | solution.py:38
  104.8 0.0 reduce-scatter.2.cloned.1.call-update
  104.8 0.0 copy-done.1
  104.8 5.9 %collective-permute-start.4 = (bf16[256,384]{1,0:T(8,128)(2,1)S(1)}, bf16[256,384]{1,0:T(8,128)(2,1)S(1)}, u32[]{:S(2)}, u32[]{:S(2)}) collective-permute-start(bf16[256,384]{1,0:T(8,128)(2,1)S(1)} %copy-done.1), channel_id=1, source_target_pairs={{0,7},{1,0},{2,1},{3,2},{4,3},{5,4},{6,5},{7,6},{8,15},{9,8},{10,9... | collective-permute-start | bytes 589832 | tf_op jit(solution)/shard_map/ppermute | solution.py:31
  110.7 0.0 collective-permute-done.1
  110.7 1.9 %collective-permute-start.2 = (bf16[256,384]{1,0:T(8,128)(2,1)S(1)}, bf16[256,384]{1,0:T(8,128)(2,1)S(1)}, u32[]{:S(2)}, u32[]{:S(2)}) collective-permute-start(bf16[256,384]{1,0:T(8,128)(2,1)S(1)} %collective-permute-done.1), channel_id=1, source_target_pairs={{0,1},{1,2},{2,3},{3,4},{4,5},{5,6},{6,7},{7,0},{8,9},{9,10},{10,1... | collective-permute-start | bytes 589832 | tf_op jit(solution)/shard_map/ppermute | solution.py:29
  112.6 2.6 %collective-permute-done.4 = bf16[256,384]{1,0:T(8,128)(2,1)S(1)} collective-permute-done((bf16[256,384]{1,0:T(8,128)(2,1)S(1)}, bf16[256,384]{1,0:T(8,128)(2,1)S(1)}, u32[]{:S(2)}, u32[]{:S(2)}) %collective-permute-start.4) | collective-permute-done | bytes 196640 | tf_op jit(solution)/shard_map/ppermute | solution.py:31
  115.2 5.6 %collective-permute-start.5 = (bf16[256,384]{1,0:T(8,128)(2,1)S(1)}, bf16[256,384]{1,0:T(8,128)(2,1)S(1)}, u32[]{:S(2)}, u32[]{:S(2)}) collective-permute-start(bf16[256,384]{1,0:T(8,128)(2,1)S(1)} %collective-permute-done.4), channel_id=1, source_target_pairs={{0,7},{1,0},{2,1},{3,2},{4,3},{5,4},{6,5},{7,6},{8,15},{9,8},{10,9... | collective-permute-start | bytes 589832 | tf_op jit(solution)/shard_map/ppermute | solution.py:31
  120.8 0.0 collective-permute-done.2
  120.8 1.9 %collective-permute-start.3 = (bf16[256,384]{1,0:T(8,128)(2,1)S(1)}, bf16[256,384]{1,0:T(8,128)(2,1)S(1)}, u32[]{:S(2)}, u32[]{:S(2)}) collective-permute-start(bf16[256,384]{1,0:T(8,128)(2,1)S(1)} %collective-permute-done.2), channel_id=1, source_target_pairs={{0,1},{1,2},{2,3},{3,4},{4,5},{5,6},{6,7},{7,0},{8,9},{9,10},{10,1... | collective-permute-start | bytes 589832 | tf_op jit(solution)/shard_map/ppermute | solution.py:29
  122.8 4.8 %collective-permute-done.5 = bf16[256,384]{1,0:T(8,128)(2,1)S(1)} collective-permute-done((bf16[256,384]{1,0:T(8,128)(2,1)S(1)}, bf16[256,384]{1,0:T(8,128)(2,1)S(1)}, u32[]{:S(2)}, u32[]{:S(2)}) %collective-permute-start.5) | collective-permute-done | bytes 196640 | tf_op jit(solution)/shard_map/ppermute | solution.py:31
  127.6 5.6 %collective-permute-start.6 = (bf16[256,384]{1,0:T(8,128)(2,1)S(1)}, bf16[256,384]{1,0:T(8,128)(2,1)S(1)}, u32[]{:S(2)}, u32[]{:S(2)}) collective-permute-start(bf16[256,384]{1,0:T(8,128)(2,1)S(1)} %collective-permute-done.5), channel_id=1, source_target_pairs={{0,7},{1,0},{2,1},{3,2},{4,3},{5,4},{6,5},{7,6},{8,15},{9,8},{10,9... | collective-permute-start | bytes 589832 | tf_op jit(solution)/shard_map/ppermute | solution.py:31
  133.2 1.0 collective-permute-done.3
  134.4 6.9 %collective-permute-done.6 = bf16[256,384]{1,0:T(8,128)(2,1)S(1)} collective-permute-done((bf16[256,384]{1,0:T(8,128)(2,1)S(1)}, bf16[256,384]{1,0:T(8,128)(2,1)S(1)}, u32[]{:S(2)}, u32[]{:S(2)}) %collective-permute-start.6) | collective-permute-done | bytes 196640 | tf_op jit(solution)/shard_map/ppermute | solution.py:31
  141.6 6.6 %convolution_convert_fusion = bf16[384,1536]{1,0:T(8,128)(2,1)} fusion(bf16[2048,1536]{1,0:T(8,128)(2,1)} %all-gather.2.cloned.1.call-done, bf16[4096,384]{1,0:T(8,128)(2,1)S(1)} %constant_dynamic-update-slice_fusion, s32[]{:T(128)S(6)} %select_n.14), kind=kOutput, calls=%fused_computation.10 | convolution fusion | flops 2424373248 | bytes 9043972 | tf_op jit(solution)/shard_map/dot_general | solution.py:35
  148.2 5.2 %reduce-scatter.2.cloned.1.call-done = bf16[256,384]{1,0:T(8,128)(2,1)} async-done(((bf16[2048,384]{1,0:T(8,128)(2,1)}), bf16[256,384]{1,0:T(8,128)(2,1)}) %reduce-scatter.2.cloned.1.call-update) | async-done | bytes 196624 | tf_op jit(solution)/shard_map/reduce_scatter | solution.py:41
  153.4 1.9 %fusion.18 = bf16[256,384]{1,0:T(8,128)(2,1)} fusion(bf16[256,384]{1,0:T(8,128)(2,1)S(1)} %copy-done.1, bf16[256,384]{1,0:T(8,128)(2,1)} %reduce-scatter.2.cloned.1.call-done), kind=kLoop, calls=%fused_computation.31 | loop fusion | flops 2064384 | bytes 589824 | tf_op jit(solution)/shard_map/convert_element_type | solution.py:44
  (16 shorter events, 0.5 us)
Async XLA Ops:
  7.2 90.2 %copy-start = (bf16[384,1536]{1,0:T(8,128)(2,1)S(1)}, bf16[384,1536]{1,0:T(8,128)(2,1)}, u32[]{:S(2)}) copy-start(bf16[384,1536]{1,0:T(8,128)(2,1)} %param.5) | copy-start | bytes 3538948
  7.2 90.2 %all-gather.2.cloned.1.call-start = ((), (), s32[]{:S(2)}) async-start(), calls=%async_computation.1 | async-start | bytes 6389760 | tf_op jit(solution)/shard_map/all_gather | solution.py:23
  7.9 96.9 %copy-start.1 = (bf16[256,384]{1,0:T(8,128)(2,1)S(1)}, bf16[256,384]{1,0:T(8,128)(2,1)}, u32[]{:S(2)}) copy-start(bf16[256,384]{1,0:T(8,128)(2,1)} %param.4) | copy-start | bytes 589828
  7.9 145.5 %reduce-scatter.2.cloned.1.call-start = ((), (), s32[]{:S(2)}) async-start(), calls=%async_computation.2 | async-start | bytes 1769472 | tf_op jit(solution)/shard_map/reduce_scatter | solution.py:41
  8.0 16.1 %collective-permute-start = (bf16[256,384]{1,0:T(8,128)(2,1)}, bf16[256,384]{1,0:T(8,128)(2,1)S(1)}, u32[]{:S(2)}, u32[]{:S(2)}) collective-permute-start(bf16[256,384]{1,0:T(8,128)(2,1)} %param.4), channel_id=1, source_target_pairs={{0,1},{1,2},{2,3},{3,4},{4,5},{5,6},{6,7},{7,0},{8,9},{9,10},{10,1... | collective-permute-start | bytes 589832 | tf_op jit(solution)/shard_map/ppermute | solution.py:29
  24.0 86.7 %collective-permute-start.1 = (bf16[256,384]{1,0:T(8,128)(2,1)S(1)}, bf16[256,384]{1,0:T(8,128)(2,1)S(1)}, u32[]{:S(2)}, u32[]{:S(2)}) collective-permute-start(bf16[256,384]{1,0:T(8,128)(2,1)S(1)} %collective-permute-done), channel_id=1, source_target_pairs={{0,1},{1,2},{2,3},{3,4},{4,5},{5,6},{6,7},{7,0},{8,9},{9,10},{10,1... | collective-permute-start | bytes 589832 | tf_op jit(solution)/shard_map/ppermute | solution.py:29
  104.8 10.4 %collective-permute-start.4 = (bf16[256,384]{1,0:T(8,128)(2,1)S(1)}, bf16[256,384]{1,0:T(8,128)(2,1)S(1)}, u32[]{:S(2)}, u32[]{:S(2)}) collective-permute-start(bf16[256,384]{1,0:T(8,128)(2,1)S(1)} %copy-done.1), channel_id=1, source_target_pairs={{0,7},{1,0},{2,1},{3,2},{4,3},{5,4},{6,5},{7,6},{8,15},{9,8},{10,9... | collective-permute-start | bytes 589832 | tf_op jit(solution)/shard_map/ppermute | solution.py:31
  110.7 10.1 %collective-permute-start.2 = (bf16[256,384]{1,0:T(8,128)(2,1)S(1)}, bf16[256,384]{1,0:T(8,128)(2,1)S(1)}, u32[]{:S(2)}, u32[]{:S(2)}) collective-permute-start(bf16[256,384]{1,0:T(8,128)(2,1)S(1)} %collective-permute-done.1), channel_id=1, source_target_pairs={{0,1},{1,2},{2,3},{3,4},{4,5},{5,6},{6,7},{7,0},{8,9},{9,10},{10,1... | collective-permute-start | bytes 589832 | tf_op jit(solution)/shard_map/ppermute | solution.py:29
  115.2 12.3 %collective-permute-start.5 = (bf16[256,384]{1,0:T(8,128)(2,1)S(1)}, bf16[256,384]{1,0:T(8,128)(2,1)S(1)}, u32[]{:S(2)}, u32[]{:S(2)}) collective-permute-start(bf16[256,384]{1,0:T(8,128)(2,1)S(1)} %collective-permute-done.4), channel_id=1, source_target_pairs={{0,7},{1,0},{2,1},{3,2},{4,3},{5,4},{6,5},{7,6},{8,15},{9,8},{10,9... | collective-permute-start | bytes 589832 | tf_op jit(solution)/shard_map/ppermute | solution.py:31
  120.8 13.3 %collective-permute-start.3 = (bf16[256,384]{1,0:T(8,128)(2,1)S(1)}, bf16[256,384]{1,0:T(8,128)(2,1)S(1)}, u32[]{:S(2)}, u32[]{:S(2)}) collective-permute-start(bf16[256,384]{1,0:T(8,128)(2,1)S(1)} %collective-permute-done.2), channel_id=1, source_target_pairs={{0,1},{1,2},{2,3},{3,4},{4,5},{5,6},{6,7},{7,0},{8,9},{9,10},{10,1... | collective-permute-start | bytes 589832 | tf_op jit(solution)/shard_map/ppermute | solution.py:29
  127.6 13.7 %collective-permute-start.6 = (bf16[256,384]{1,0:T(8,128)(2,1)S(1)}, bf16[256,384]{1,0:T(8,128)(2,1)S(1)}, u32[]{:S(2)}, u32[]{:S(2)}) collective-permute-start(bf16[256,384]{1,0:T(8,128)(2,1)S(1)} %collective-permute-done.5), channel_id=1, source_target_pairs={{0,7},{1,0},{2,1},{3,2},{4,3},{5,4},{6,5},{7,6},{8,15},{9,8},{10,9... | collective-permute-start | bytes 589832 | tf_op jit(solution)/shard_map/ppermute | solution.py:31
Sparse Core Ops, SparseCore 0:
  11.3 86.0 all-gather.1
  104.9 48.4 reduce-scatter.1
